TPU v7x, 256 devices: a whole 4x4x8 slice. The times are simulated.
256 devices in a mesh: gx: 16 (over z, core), gy: 16 (over y, x).
Axes of the slice: x: 4, y: 4, z: 8, core: 2. Of those that a mesh axis runs over, the one named last changes fastest.
Arguments:
- right_side: float32 [256, 128, 1024], P('gx', 'gy'), may hold values from -340 to 340
- start_guess: float32 [256, 128, 1024], P('gx', 'gy'), may hold values from -1.8 to 1.8
- couple_x: float32 [256, 128, 64], P('gx', 'gy'), may hold values from 0.3 to 3
- couple_y: float32 [256, 128, 64], P('gx', 'gy'), may hold values from 0.3 to 3
- couple_z: float32 [256, 128, 64], P('gx', 'gy'), may hold values from 0.3 to 3
- reaction: float32 [256, 128, 64], P('gx', 'gy'), may hold values from 0.01 to 0.1
Outputs:
- solution: float32 [256, 128, 1024], P('gx', 'gy')
- residual: float32 [256, 128, 1024], P('gx', 'gy')
All inputs are finite; a program needn't handle non-finite values.
Results may differ from a plain program's by a relative error of at most 0.0003.
Values sent between devices are 32-bit elements; how exact they have to be, the bound alone decides.
No kernel may reach another device: no remote copies, remote signals or barrier semaphores. Data moves between devices by JAX's collectives and lax.ppermute only.
A program may use at most 64 MiB of HBM per device.

v0:
```python
import jax
import jax.numpy as jnp
from jax import lax
from jax.sharding import PartitionSpec as P

ITERS = 2
SWEEPS = 4
FACT_SWEEPS = 3
HIGH = lax.Precision.HIGHEST


def passed_along(block, axis, distance):
    devices = range(lax.axis_size(axis))
    route = [(i - distance, i) for i in devices if i - distance in devices]
    return lax.ppermute(block, axis, route)


def padded_2(block, sides, width):
    for axis, dim in sides:
        count = lax.axis_size(axis)
        forward = [(i, i + 1) for i in range(count - 1)]
        backward = [(target, source) for source, target in forward]
        low = lax.ppermute(
            lax.slice_in_dim(block, block.shape[dim] - width, None, axis=dim), axis, forward
        )
        high = lax.ppermute(lax.slice_in_dim(block, 0, width, axis=dim), axis, backward)
        block = jnp.concatenate([low, block, high], axis=dim)
    return block


def low_shift(values, along):
    count = values.shape[along]
    blank = jnp.zeros_like(lax.slice_in_dim(values, 0, 1, axis=along))
    return jnp.concatenate([blank, lax.slice_in_dim(values, 0, count - 1, axis=along)], axis=along)


def up_shift(values, along):
    count = values.shape[along]
    blank = jnp.zeros_like(lax.slice_in_dim(values, 0, 1, axis=along))
    return jnp.concatenate([lax.slice_in_dim(values, 1, count, axis=along), blank], axis=along)


def block_gram(former, latter, count_rhs):
    cells = former.shape[0] * former.shape[1]
    left = former.reshape(cells, count_rhs, -1)
    right = latter.reshape(cells, count_rhs, -1)
    return jnp.einsum("psz,ptz->st", left, right, precision=HIGH)


def mix_block(values, matrix):
    rows_x, rows_y, flat_len = values.shape
    count_rhs = matrix.shape[0]
    split = values.reshape(rows_x * rows_y, count_rhs, flat_len // count_rhs)
    return jnp.einsum("psz,st->ptz", split, matrix, precision=HIGH).reshape(
        rows_x, rows_y, flat_len
    )


def chol_factor(gram_mat):
    low_factor = jnp.linalg.cholesky(gram_mat)
    eye_mat = jnp.eye(gram_mat.shape[0], dtype=gram_mat.dtype)
    inverse = lax.linalg.triangular_solve(low_factor, eye_mat, left_side=True, lower=True)
    return (low_factor.T, inverse.T)


def solve_small(columns, first_factor):
    hessen = jnp.concatenate(columns, axis=1)
    count_rhs = first_factor.shape[0]
    target = jnp.dot(hessen[:count_rhs].T, first_factor, precision=HIGH)
    normal = jnp.dot(hessen.T, hessen, precision=HIGH)
    low_factor = jnp.linalg.cholesky(normal)
    partial_sol = lax.linalg.triangular_solve(low_factor, target, left_side=True, lower=True)
    return lax.linalg.triangular_solve(
        low_factor, partial_sol, left_side=True, lower=True, transpose_a=True
    )


def body(right_side, start_guess, couple_x, couple_y, couple_z, reaction):
    rows_x, rows_y, flat_len = right_side.shape
    layers = couple_z.shape[2]
    count_rhs = flat_len // layers
    depth = jnp.arange(flat_len, dtype=jnp.int32) % layers
    keep_first = (depth != 0).astype(jnp.float32)
    keep_last = (depth != layers - 1).astype(jnp.float32)

    def low_z(values):
        return low_shift(values, 2) * keep_first

    def up_z(values):
        return up_shift(values, 2) * keep_last

    def tiled(values):
        return jnp.tile(values, (1, 1, count_rhs))

    edge_x = passed_along(couple_x[-1:], "gx", 1)
    edge_y = passed_along(couple_y[:, -1:], "gy", 1)
    after_x = tiled(couple_x)
    after_y = tiled(couple_y)
    after_z = tiled(couple_z)
    before_x = tiled(jnp.concatenate([edge_x, couple_x[:-1]], axis=0))
    before_y = tiled(jnp.concatenate([edge_y, couple_y[:, :-1]], axis=1))
    before_z = low_z(after_z)
    diagonal = tiled(reaction) + after_x + before_x + after_y + before_y + after_z + before_z

    def apply_op(values):
        padded = padded_2(values, (("gx", 0), ("gy", 1)), 1)
        centre = padded[1:-1, 1:-1]
        return (
            diagonal * centre
            - after_x * padded[2:, 1:-1]
            - before_x * padded[:-2, 1:-1]
            - after_y * padded[1:-1, 2:]
            - before_y * padded[1:-1, :-2]
            - after_z * up_z(centre)
            - before_z * low_z(centre)
        )

    lows = (low_shift(after_x, 0), low_shift(after_y, 1), before_z)
    ups = (
        up_shift(jnp.ones_like(after_x), 0) * after_x,
        up_shift(jnp.ones_like(after_y), 1) * after_y,
        after_z,
    )
    pivots = diagonal
    for repeat in range(FACT_SWEEPS):
        inv_now = 1.0 / pivots
        pivots = (
            diagonal
            - lows[0] * lows[0] * low_shift(inv_now, 0)
            - lows[1] * lows[1] * low_shift(inv_now, 1)
            - lows[2] * lows[2] * low_z(inv_now)
        )
    inv_piv = 1.0 / pivots

    def total_gram(former, latter):
        return lax.psum(block_gram(former, latter, count_rhs), ("gx", "gy"))

    start_res = right_side - apply_op(start_guess)
    first_factor, first_inv = chol_factor(total_gram(start_res, start_res))
    basis_set = [mix_block(start_res, first_inv)]
    precond_set = []
    image_set = []
    columns = []
    for column in range(ITERS):
        source = basis_set[column]
        lower_sol = inv_piv * source
        for precondition_repeat in range(SWEEPS):
            lower_sol = inv_piv * (
                source
                + lows[0] * low_shift(lower_sol, 0)
                + lows[1] * low_shift(lower_sol, 1)
                + lows[2] * low_z(lower_sol)
            )
        upper_sol = lower_sol
        for precondition_repeat in range(SWEEPS):
            upper_sol = lower_sol + inv_piv * (
                ups[0] * up_shift(upper_sol, 0)
                + ups[1] * up_shift(upper_sol, 1)
                + ups[2] * up_z(upper_sol)
            )
        image = apply_op(upper_sol)
        precond_set.append(upper_sol)
        image_set.append(image)
        local_proj = jnp.stack([block_gram(member, image, count_rhs) for member in basis_set])
        stacked = lax.psum(local_proj, ("gx", "gy"))
        projections = [stacked[member] for member in range(len(basis_set))]
        removed = mix_block(basis_set[0], projections[0])
        for member in range(1, len(basis_set)):
            removed = removed + mix_block(basis_set[member], projections[member])
        perp = image - removed
        next_factor, next_inv = chol_factor(total_gram(perp, perp))
        if column + 1 < ITERS:
            basis_set.append(mix_block(perp, next_inv))
        blank = jnp.zeros(((ITERS - 1 - column) * count_rhs, count_rhs), dtype=next_factor.dtype)
        columns.append(jnp.concatenate(projections + [next_factor, blank], axis=0))
    coeffs = solve_small(columns, first_factor)
    solution = start_guess
    for column in range(ITERS):
        solution = solution + mix_block(
            precond_set[column], coeffs[column * count_rhs : (column + 1) * count_rhs]
        )
    residual = right_side - apply_op(solution)
    return (solution, residual)


def solution(mesh):
    return jax.shard_map(
        body,
        mesh=mesh,
        in_specs=(
            P("gx", "gy", None),
            P("gx", "gy", None),
            P("gx", "gy", None),
            P("gx", "gy", None),
            P("gx", "gy", None),
            P("gx", "gy", None),
        ),
        out_specs=(P("gx", "gy", None), P("gx", "gy", None)),
        check_vma=False,
    )
```

profile of v0, /device:TPU:40, one launch (start us, length us, event | category | flops | bytes accessed | tf_op | source)
XLA Modules:
  0.0 608.5 jit_solution(9430777300080090725)
XLA Ops:
  3.4 3.6 collective-permute-start.2
  9.3 3.4 collective-permute-start.1
  29.7 4.6 collective-permute-start.4
  39.6 3.6 collective-permute-done.5
  43.2 3.8 fusion.36
  49.3 3.1 convolution_bitcast_fusion.12
  57.6 77.3 %psum.35 = f32[16,16]{0,1:T(8,128)S(1)} all-reduce(f32[16,16]{0,1:T(8,128)S(1)} %convolution_bitcast_fusion.12), channel_id=1, replica_groups=mesh['gx'=16,'gy'=16] {'gx','gy'}, use_global_device_ids=true, to_apply=%region_0.1 | all-reduce | flops 256 | bytes 2048 | tf_op jit(solution)/shard_map/psum | solution.py:136
  153.0 2.8 collective-permute-start.6
  157.7 3.3 collective-permute-done.7
  161.1 4.6 collective-permute-start.8
  168.1 6.2 %collective-permute-done.9 = f32[18,1,1024]{2,1,0:T(1,128)S(1)} collective-permute-done((f32[18,1,1024]{2,1,0:T(1,128)S(1)}, f32[18,1,1024]{2,1,0:T(1,128)S(1)}, u32[]{:S(2)}, u32[]{:S(2)}) %collective-permute-start.9) | collective-permute-done | bytes 73760 | tf_op jit(solution)/shard_map/ppermute | solution.py:23
  182.5 71.4 %psum.36 = f32[16,16]{0,1:T(8,128)S(1)} all-reduce(f32[16,16]{0,1:T(8,128)S(1)} %convolution_bitcast_fusion.10), channel_id=1, replica_groups=mesh['gx'=16,'gy'=16] {'gx','gy'}, use_global_device_ids=true, to_apply=%region_3.6 | all-reduce | flops 256 | bytes 2048 | tf_op jit(solution)/shard_map/psum | solution.py:165
  268.0 3.1 convolution_bitcast_fusion.9
  271.0 74.0 %psum.37 = f32[16,16]{0,1:T(8,128)S(1)} all-reduce(f32[16,16]{0,1:T(8,128)S(1)} %convolution_bitcast_fusion.9), channel_id=1, replica_groups=mesh['gx'=16,'gy'=16] {'gx','gy'}, use_global_device_ids=true, to_apply=%region_4.7 | all-reduce | flops 256 | bytes 2048 | tf_op jit(solution)/shard_map/psum | solution.py:136
  364.9 2.9 collective-permute-start.10
  375.0 4.6 collective-permute-start.12
  388.1 2.9 fusion.15
  398.7 75.0 %psum.38 = f32[2,16,16]{1,2,0:T(8,128)S(1)} all-reduce(f32[2,16,16]{1,2,0:T(8,128)S(1)} %pad_maximum_fusion.39), channel_id=1, replica_groups=mesh['gx'=16,'gy'=16] {'gx','gy'}, use_global_device_ids=true, to_apply=%region_5.8 | all-reduce | flops 512 | bytes 4096 | tf_op jit(solution)/shard_map/psum | solution.py:165
  483.3 3.1 convolution_bitcast_fusion.5
  486.5 74.9 %psum.39 = f32[16,16]{0,1:T(8,128)S(1)} all-reduce(f32[16,16]{0,1:T(8,128)S(1)} %convolution_bitcast_fusion.5), channel_id=1, replica_groups=mesh['gx'=16,'gy'=16] {'gx','gy'}, use_global_device_ids=true, to_apply=%region_6.9 | all-reduce | flops 256 | bytes 2048 | tf_op jit(solution)/shard_map/psum | solution.py:136
  565.4 2.9 cholesky.41
  590.7 2.8 collective-permute-done.15
  593.6 4.7 collective-permute-start.16
  600.6 6.2 %collective-permute-done.17 = f32[18,1,1024]{2,1,0:T(1,128)S(1)} collective-permute-done((f32[18,1,1024]{2,1,0:T(1,128)S(1)}, f32[18,1,1024]{2,1,0:T(1,128)S(1)}, u32[]{:S(2)}, u32[]{:S(2)}) %collective-permute-start.17) | collective-permute-done | bytes 73760 | tf_op jit(solution)/shard_map/ppermute | solution.py:23
  (248 shorter events, 161.8 us)
Async XLA Ops:
  0.6 8.6 %copy-start.23 = (f32[16,8,64]{2,1,0:T(8,128)S(1)}, f32[16,8,64]{2,1,0:T(8,128)}, u32[]{:S(2)}) copy-start(f32[16,8,64]{2,1,0:T(8,128)} %param.12) | copy-start | bytes 98308
  1.5 27.3 %collective-permute-start.3 = (f32[1,8,1024]{2,1,0:T(8,128)S(1)}, f32[1,8,1024]{2,1,0:T(8,128)S(1)}, u32[]{:S(2)}, u32[]{:S(2)}) collective-permute-start(f32[1,8,1024]{2,1,0:T(8,128)S(1)} %get-tuple-element.31), channel_id=1, source_target_pairs={{0,16},{16,32},{32,48},{48,64},{64,80},{80,96},{96,112},{112,128},... | collective-permute-start | bytes 98312 | tf_op jit(solution)/shard_map/ppermute | solution.py:23
  3.4 25.4 %collective-permute-start.2 = (f32[1,8,1024]{2,1,0:T(8,128)S(1)}, f32[1,8,1024]{2,1,0:T(8,128)S(1)}, u32[]{:S(2)}, u32[]{:S(2)}) collective-permute-start(f32[1,8,1024]{2,1,0:T(8,128)S(1)} %get-tuple-element.30), channel_id=1, source_target_pairs={{16,0},{32,16},{48,32},{64,48},{80,64},{96,80},{112,96},{128,112},... | collective-permute-start | bytes 98312 | tf_op jit(solution)/shard_map/ppermute | solution.py:26
  7.1 18.2 %collective-permute-start = (f32[1,8,64]{2,1,0:T(8,128)S(1)}, f32[1,8,64]{2,1,0:T(8,128)S(1)}, u32[]{:S(2)}, u32[]{:S(2)}) collective-permute-start(f32[1,8,64]{2,1,0:T(8,128)S(1)} %slice.369), channel_id=1, source_target_pairs={{0,16},{16,32},{32,48},{48,64},{64,80},{80,96},{96,112},{112,128},... | collective-permute-start | bytes 6152 | tf_op jit(solution)/shard_map/ppermute | solution.py:15
  9.3 26.9 %collective-permute-start.1 = (f32[16,1,64]{2,1,0:T(1,128)S(1)}, f32[16,1,64]{2,1,0:T(1,128)S(1)}, u32[]{:S(2)}, u32[]{:S(2)}) collective-permute-start(f32[16,1,64]{2,1,0:T(1,128)S(1)} %slice.371), channel_id=1, source_target_pairs={{0,1},{1,2},{2,3},{3,4},{4,5},{5,6},{6,7},{7,8},{8,9},{9,10},{10,1... | collective-permute-start | bytes 12296 | tf_op jit(solution)/shard_map/ppermute | solution.py:15
  29.7 9.9 %collective-permute-start.4 = (f32[18,1,1024]{2,1,0:T(1,128)S(1)}, f32[18,1,1024]{2,1,0:T(1,128)S(1)}, u32[]{:S(2)}, u32[]{:S(2)}) collective-permute-start(f32[18,1,1024]{2,1,0:T(1,128)S(1)} %get-tuple-element.14), channel_id=1, source_target_pairs={{1,0},{2,1},{3,2},{4,3},{5,4},{6,5},{7,6},{8,7},{9,8},{10,9},{11,1... | collective-permute-start | bytes 221192 | tf_op jit(solution)/shard_map/ppermute | solution.py:26
  34.3 8.9 %collective-permute-start.5 = (f32[18,1,1024]{2,1,0:T(1,128)S(1)}, f32[18,1,1024]{2,1,0:T(1,128)S(1)}, u32[]{:S(2)}, u32[]{:S(2)}) collective-permute-start(f32[18,1,1024]{2,1,0:T(1,128)S(1)} %get-tuple-element.15), channel_id=1, source_target_pairs={{0,1},{1,2},{2,3},{3,4},{4,5},{5,6},{6,7},{7,8},{8,9},{9,10},{10,1... | collective-permute-start | bytes 221192 | tf_op jit(solution)/shard_map/ppermute | solution.py:23
  152.9 21.3 %copy-start = (f32[16,8,1024]{2,1,0:T(8,128)}, f32[16,8,1024]{2,1,0:T(8,128)S(1)}, u32[]{:S(2)}) copy-start(f32[16,8,1024]{2,1,0:T(8,128)S(1)} %multiply_add_fusion.4) | copy-start | bytes 1572868
  153.0 4.8 collective-permute-start.6
  155.8 5.2 collective-permute-start.7
  161.1 6.9 %collective-permute-start.8 = (f32[18,1,1024]{2,1,0:T(1,128)S(1)}, f32[18,1,1024]{2,1,0:T(1,128)S(1)}, u32[]{:S(2)}, u32[]{:S(2)}) collective-permute-start(f32[18,1,1024]{2,1,0:T(1,128)S(1)} %get-tuple-element.12), channel_id=1, source_target_pairs={{1,0},{2,1},{3,2},{4,3},{5,4},{6,5},{7,6},{8,7},{9,8},{10,9},{11,1... | collective-permute-start | bytes 221192 | tf_op jit(solution)/shard_map/ppermute | solution.py:26
  165.8 8.5 %collective-permute-start.9 = (f32[18,1,1024]{2,1,0:T(1,128)S(1)}, f32[18,1,1024]{2,1,0:T(1,128)S(1)}, u32[]{:S(2)}, u32[]{:S(2)}) collective-permute-start(f32[18,1,1024]{2,1,0:T(1,128)S(1)} %get-tuple-element.13), channel_id=1, source_target_pairs={{0,1},{1,2},{2,3},{3,4},{4,5},{5,6},{6,7},{7,8},{8,9},{9,10},{10,1... | collective-permute-start | bytes 221192 | tf_op jit(solution)/shard_map/ppermute | solution.py:23
  364.9 10.0 %collective-permute-start.10 = (f32[1,8,1024]{2,1,0:T(8,128)S(1)}, f32[1,8,1024]{2,1,0:T(8,128)S(1)}, u32[]{:S(2)}, u32[]{:S(2)}) collective-permute-start(f32[1,8,1024]{2,1,0:T(8,128)S(1)} %get-tuple-element.23), channel_id=1, source_target_pairs={{16,0},{32,16},{48,32},{64,48},{80,64},{96,80},{112,96},{128,112},... | collective-permute-start | bytes 98312 | tf_op jit(solution)/shard_map/ppermute | solution.py:26
  367.9 7.0 %collective-permute-start.11 = (f32[1,8,1024]{2,1,0:T(8,128)S(1)}, f32[1,8,1024]{2,1,0:T(8,128)S(1)}, u32[]{:S(2)}, u32[]{:S(2)}) collective-permute-start(f32[1,8,1024]{2,1,0:T(8,128)S(1)} %get-tuple-element.22), channel_id=1, source_target_pairs={{0,16},{16,32},{32,48},{48,64},{64,80},{80,96},{96,112},{112,128},... | collective-permute-start | bytes 98312 | tf_op jit(solution)/shard_map/ppermute | solution.py:23
  375.0 11.5 %collective-permute-start.12 = (f32[18,1,1024]{2,1,0:T(1,128)S(1)}, f32[18,1,1024]{2,1,0:T(1,128)S(1)}, u32[]{:S(2)}, u32[]{:S(2)}) collective-permute-start(f32[18,1,1024]{2,1,0:T(1,128)S(1)} %get-tuple-element.10), channel_id=1, source_target_pairs={{1,0},{2,1},{3,2},{4,3},{5,4},{6,5},{7,6},{8,7},{9,8},{10,9},{11,1... | collective-permute-start | bytes 221192 | tf_op jit(solution)/shard_map/ppermute | solution.py:26
  379.6 8.4 %collective-permute-start.13 = (f32[18,1,1024]{2,1,0:T(1,128)S(1)}, f32[18,1,1024]{2,1,0:T(1,128)S(1)}, u32[]{:S(2)}, u32[]{:S(2)}) collective-permute-start(f32[18,1,1024]{2,1,0:T(1,128)S(1)} %get-tuple-element.11), channel_id=1, source_target_pairs={{0,1},{1,2},{2,3},{3,4},{4,5},{5,6},{6,7},{7,8},{8,9},{9,10},{10,1... | collective-permute-start | bytes 221192 | tf_op jit(solution)/shard_map/ppermute | solution.py:23
  483.3 89.2 %copy-start.20 = (f32[128,16,64]{0,1,2:T(8,128)S(1)}, f32[128,16,64]{0,1,2:T(8,128)}, u32[]{:S(2)}) copy-start(f32[128,16,64]{0,1,2:T(8,128)} %copy.56) | copy-start | bytes 1572868
  586.3 20.5 %copy-start.9 = (f32[16,8,1024]{2,1,0:T(8,128)}, f32[16,8,1024]{2,1,0:T(8,128)S(1)}, u32[]{:S(2)}) copy-start(f32[16,8,1024]{2,1,0:T(8,128)S(1)} %add_add_fusion) | copy-start | bytes 1572868
  586.3 4.3 collective-permute-start.14
  588.3 5.2 collective-permute-start.15
  593.6 7.0 %collective-permute-start.16 = (f32[18,1,1024]{2,1,0:T(1,128)S(1)}, f32[18,1,1024]{2,1,0:T(1,128)S(1)}, u32[]{:S(2)}, u32[]{:S(2)}) collective-permute-start(f32[18,1,1024]{2,1,0:T(1,128)S(1)} %get-tuple-element.8), channel_id=1, source_target_pairs={{1,0},{2,1},{3,2},{4,3},{5,4},{6,5},{7,6},{8,7},{9,8},{10,9},{11,1... | collective-permute-start | bytes 221192 | tf_op jit(solution)/shard_map/ppermute | solution.py:26
  598.2 8.5 %copy-start.11 = (f32[16,8,1024]{2,1,0:T(8,128)S(1)}, f32[16,8,1024]{2,1,0:T(8,128)}, u32[]{:S(2)}) copy-start(f32[16,8,1024]{2,1,0:T(8,128)} %tile.63) | copy-start | bytes 1572868
  598.3 8.5 %copy-start.13 = (f32[16,8,1024]{2,1,0:T(8,128)S(1)}, f32[16,8,1024]{2,1,0:T(8,128)}, u32[]{:S(2)}) copy-start(f32[16,8,1024]{2,1,0:T(8,128)} %tile.67) | copy-start | bytes 1572868
  598.3 8.5 %collective-permute-start.17 = (f32[18,1,1024]{2,1,0:T(1,128)S(1)}, f32[18,1,1024]{2,1,0:T(1,128)S(1)}, u32[]{:S(2)}, u32[]{:S(2)}) collective-permute-start(f32[18,1,1024]{2,1,0:T(1,128)S(1)} %get-tuple-element.9), channel_id=1, source_target_pairs={{0,1},{1,2},{2,3},{3,4},{4,5},{5,6},{6,7},{7,8},{8,9},{9,10},{10,1... | collective-permute-start | bytes 221192 | tf_op jit(solution)/shard_map/ppermute | solution.py:23
  (21 other events, 59.9 us)
where the time goes:
time: 617 us; the launch traced here: 609 us
  blocking collectives  373 us (60%)
  local copies, waits for them, and re-layouts  87.7 us (14%)
  starting transfers between devices  51.7 us (8%)
  other arithmetic  44.9 us (7%)
  matrix products  26 us (4%)
  waiting for transfers between devices  23.7 us (4%)
    psum x3, blocking collectives, total_gram(): return lax.psum(block_gram(former, latter, count_rhs), ('gx', 'gy'))  226 us
    psum x2, blocking collectives, body(): stacked = lax.psum(local_proj, ('gx', 'gy'))  146 us
    ppermute x8, starting transfers between devices, padded_2(): lax.ppermute(lax.slice_in_dim(block, 0, width, axis=dim), axis, backward)  29.8 us
    ppermute x8, waiting for transfers between devices, padded_2(): lax.ppermute(lax.slice_in_dim(block, block.shape[dim] - width, None, axis...  23.7 us
    ppermute x8, starting transfers between devices, padded_2(): lax.ppermute(lax.slice_in_dim(block, block.shape[dim] - width, None, axis...  16.3 us
    another operation x14, local copies, waits for them, and re-layouts, tiled(): return jnp.tile(values, (1, 1, count_rhs))  16.1 us
    dot_general x6, matrix products, block_gram(): return jnp.einsum('psz,ptz->st', left, right, precision=HIGH)  14 us
  transfers between devices with their start and end apart: 18, of which 6 were waited for; matrix products, arithmetic and copies ran while one was open for 5% of the time, Pallas kernels for 0%

commit v1 on v0

--- a/solution.py
+++ b/solution.py
@@ -7,6 +7,14 @@
 SWEEPS = 4
 FACT_SWEEPS = 3
 HIGH = lax.Precision.HIGHEST
+
+
+def end_lanes(buf):
+    along_axis = "gx"
+    which_axis = "gy"
+    for no in (which_axis, along_axis):
+        buf = lax.psum(buf, no)
+    return buf
 
 
 def passed_along(block, axis, distance):
@@ -133,7 +141,7 @@
     inv_piv = 1.0 / pivots
 
     def total_gram(former, latter):
-        return lax.psum(block_gram(former, latter, count_rhs), ("gx", "gy"))
+        return end_lanes(block_gram(former, latter, count_rhs))
 
     start_res = right_side - apply_op(start_guess)
     first_factor, first_inv = chol_factor(total_gram(start_res, start_res))

time: 617 us -> 567 us (0.919)
  blocking collectives: 373 us -> 316 us
  starting transfers between devices: 51.7 us -> 59.1 us
    psum x3 -> x6, blocking collectives: 226 us -> 165 us  [end_lanes(): buf = lax.psum(buf, no)]
    ppermute x8, starting transfers between devices: 29.8 us -> 36.6 us  [padded_2(): lax.ppermute(lax.slice_in_dim(block, 0, width, axis=dim), axis, backward)]
where the time goes in v1:
time: 567 us; the launch traced here: 558 us
  blocking collectives  316 us (56%)
  local copies, waits for them, and re-layouts  87.9 us (16%)
  starting transfers between devices  59.1 us (10%)
  other arithmetic  44.5 us (8%)
  matrix products  26 us (5%)
  waiting for transfers between devices  22.9 us (4%)
    psum x6, blocking collectives, end_lanes(): buf = lax.psum(buf, no)  165 us
    psum x2, blocking collectives, body(): stacked = lax.psum(local_proj, ('gx', 'gy'))  150 us
    ppermute x8, starting transfers between devices, padded_2(): lax.ppermute(lax.slice_in_dim(block, 0, width, axis=dim), axis, backward)  36.6 us
    ppermute x8, waiting for transfers between devices, padded_2(): lax.ppermute(lax.slice_in_dim(block, block.shape[dim] - width, None, axis...  22.8 us
    ppermute x8, starting transfers between devices, padded_2(): lax.ppermute(lax.slice_in_dim(block, block.shape[dim] - width, None, axis...  16.9 us
    another operation x14, local copies, waits for them, and re-layouts, tiled(): return jnp.tile(values, (1, 1, count_rhs))  16.1 us
    dot_general x6, matrix products, block_gram(): return jnp.einsum('psz,ptz->st', left, right, precision=HIGH)  13.9 us
    reshape x5, local copies, waits for them, and re-layouts, block_gram(): left = former.reshape(cells, count_rhs, -1)  11.9 us
  transfers between devices with their start and end apart: 18, of which 6 were waited for; matrix products, arithmetic and copies ran while one was open for 5% of the time, Pallas kernels for 0%

profile of v1, /device:TPU:40, one launch (start us, length us, event | category | flops | bytes accessed | tf_op | source)
XLA Modules:
  0.0 558.1 jit_solution(18128831431237278926)
XLA Ops:
  3.4 3.6 collective-permute-start.2
  9.3 3.4 collective-permute-start.1
  29.8 4.6 collective-permute-start.4
  39.7 3.6 collective-permute-done.5
  43.3 3.8 fusion.36
  57.7 31.7 %psum.56 = f32[16,16]{0,1:T(8,128)S(1)} all-reduce(f32[16,16]{0,1:T(8,128)S(1)} %convolution_bitcast_fusion.12), channel_id=1, replica_groups=mesh['gx'=16,'gy'=16] {'gy'}, use_global_device_ids=true, to_apply=%region_0.1 | all-reduce | flops 256 | bytes 2048 | tf_op jit(solution)/shard_map/psum | solution.py:16
  89.4 23.2 %psum.57 = f32[16,16]{0,1:T(8,128)S(1)} all-reduce(f32[16,16]{0,1:T(8,128)S(1)} %psum.56), channel_id=1, replica_groups=mesh['gx'=16,'gy'=16] {'gx'}, use_global_device_ids=true, to_apply=%region_1.2 | all-reduce | flops 256 | bytes 2048 | tf_op jit(solution)/shard_map/psum | solution.py:16
  130.6 5.4 collective-permute-start.6
  137.9 3.3 collective-permute-done.7
  144.2 3.2 collective-permute-start.9
  147.6 5.1 collective-permute-done.9
  160.9 75.1 %psum.58 = f32[16,16]{0,1:T(8,128)S(1)} all-reduce(f32[16,16]{0,1:T(8,128)S(1)} %convolution_bitcast_fusion.10), channel_id=1, replica_groups=mesh['gx'=16,'gy'=16] {'gx','gy'}, use_global_device_ids=true, to_apply=%region_4.7 | all-reduce | flops 256 | bytes 2048 | tf_op jit(solution)/shard_map/psum | solution.py:173
  253.2 33.9 %psum.59 = f32[16,16]{0,1:T(8,128)S(1)} all-reduce(f32[16,16]{0,1:T(8,128)S(1)} %convolution_bitcast_fusion.9), channel_id=1, replica_groups=mesh['gx'=16,'gy'=16] {'gy'}, use_global_device_ids=true, to_apply=%region_5.8 | all-reduce | flops 256 | bytes 2048 | tf_op jit(solution)/shard_map/psum | solution.py:16
  287.1 20.8 %psum.60 = f32[16,16]{0,1:T(8,128)S(1)} all-reduce(f32[16,16]{0,1:T(8,128)S(1)} %psum.59), channel_id=1, replica_groups=mesh['gx'=16,'gy'=16] {'gx'}, use_global_device_ids=true, to_apply=%region_6.9 | all-reduce | flops 256 | bytes 2048 | tf_op jit(solution)/shard_map/psum | solution.py:16
  327.6 5.0 collective-permute-start.10
  339.5 6.0 %collective-permute-start.12 = (f32[18,1,1024]{2,1,0:T(1,128)S(1)}, f32[18,1,1024]{2,1,0:T(1,128)S(1)}, u32[]{:S(2)}, u32[]{:S(2)}) collective-permute-start(f32[18,1,1024]{2,1,0:T(1,128)S(1)} %get-tuple-element.10), channel_id=1, source_target_pairs={{1,0},{2,1},{3,2},{4,3},{5,4},{6,5},{7,6},{8,7},{9,8},{10,9},{11,1... | collective-permute-start | bytes 221192 | tf_op jit(solution)/shard_map/ppermute | solution.py:34
  364.5 75.3 %psum.61 = f32[2,16,16]{1,2,0:T(8,128)S(1)} all-reduce(f32[2,16,16]{1,2,0:T(8,128)S(1)} %pad_maximum_fusion.39), channel_id=1, replica_groups=mesh['gx'=16,'gy'=16] {'gx','gy'}, use_global_device_ids=true, to_apply=%region_7.10 | all-reduce | flops 512 | bytes 4096 | tf_op jit(solution)/shard_map/psum | solution.py:173
  449.5 3.1 convolution_bitcast_fusion.5
  452.6 33.9 %psum.62 = f32[16,16]{0,1:T(8,128)S(1)} all-reduce(f32[16,16]{0,1:T(8,128)S(1)} %convolution_bitcast_fusion.5), channel_id=1, replica_groups=mesh['gx'=16,'gy'=16] {'gy'}, use_global_device_ids=true, to_apply=%region_8.11 | all-reduce | flops 256 | bytes 2048 | tf_op jit(solution)/shard_map/psum | solution.py:16
  486.5 21.9 %psum.63 = f32[16,16]{0,1:T(8,128)S(1)} all-reduce(f32[16,16]{0,1:T(8,128)S(1)} %psum.62), channel_id=1, replica_groups=mesh['gx'=16,'gy'=16] {'gx'}, use_global_device_ids=true, to_apply=%region_9.12 | all-reduce | flops 256 | bytes 2048 | tf_op jit(solution)/shard_map/psum | solution.py:16
  533.2 4.8 collective-permute-start.14
  540.0 3.3 collective-permute-done.15
  543.4 4.4 collective-permute-start.16
  550.2 6.2 %collective-permute-done.17 = f32[18,1,1024]{2,1,0:T(1,128)S(1)} collective-permute-done((f32[18,1,1024]{2,1,0:T(1,128)S(1)}, f32[18,1,1024]{2,1,0:T(1,128)S(1)}, u32[]{:S(2)}, u32[]{:S(2)}) %collective-permute-start.17) | collective-permute-done | bytes 73760 | tf_op jit(solution)/shard_map/ppermute | solution.py:31
  (251 shorter events, 171.6 us)
Async XLA Ops:
  0.6 8.6 %copy-start.23 = (f32[16,8,64]{2,1,0:T(8,128)S(1)}, f32[16,8,64]{2,1,0:T(8,128)}, u32[]{:S(2)}) copy-start(f32[16,8,64]{2,1,0:T(8,128)} %param.12) | copy-start | bytes 98308
  1.5 27.3 %collective-permute-start.3 = (f32[1,8,1024]{2,1,0:T(8,128)S(1)}, f32[1,8,1024]{2,1,0:T(8,128)S(1)}, u32[]{:S(2)}, u32[]{:S(2)}) collective-permute-start(f32[1,8,1024]{2,1,0:T(8,128)S(1)} %get-tuple-element.31), channel_id=1, source_target_pairs={{0,16},{16,32},{32,48},{48,64},{64,80},{80,96},{96,112},{112,128},... | collective-permute-start | bytes 98312 | tf_op jit(solution)/shard_map/ppermute | solution.py:31
  3.4 25.5 %collective-permute-start.2 = (f32[1,8,1024]{2,1,0:T(8,128)S(1)}, f32[1,8,1024]{2,1,0:T(8,128)S(1)}, u32[]{:S(2)}, u32[]{:S(2)}) collective-permute-start(f32[1,8,1024]{2,1,0:T(8,128)S(1)} %get-tuple-element.30), channel_id=1, source_target_pairs={{16,0},{32,16},{48,32},{64,48},{80,64},{96,80},{112,96},{128,112},... | collective-permute-start | bytes 98312 | tf_op jit(solution)/shard_map/ppermute | solution.py:34
  7.1 18.3 %collective-permute-start = (f32[1,8,64]{2,1,0:T(8,128)S(1)}, f32[1,8,64]{2,1,0:T(8,128)S(1)}, u32[]{:S(2)}, u32[]{:S(2)}) collective-permute-start(f32[1,8,64]{2,1,0:T(8,128)S(1)} %slice.369), channel_id=1, source_target_pairs={{0,16},{16,32},{32,48},{48,64},{64,80},{80,96},{96,112},{112,128},... | collective-permute-start | bytes 6152 | tf_op jit(solution)/shard_map/ppermute | solution.py:23
  9.3 27.0 %collective-permute-start.1 = (f32[16,1,64]{2,1,0:T(1,128)S(1)}, f32[16,1,64]{2,1,0:T(1,128)S(1)}, u32[]{:S(2)}, u32[]{:S(2)}) collective-permute-start(f32[16,1,64]{2,1,0:T(1,128)S(1)} %slice.371), channel_id=1, source_target_pairs={{0,1},{1,2},{2,3},{3,4},{4,5},{5,6},{6,7},{7,8},{8,9},{9,10},{10,1... | collective-permute-start | bytes 12296 | tf_op jit(solution)/shard_map/ppermute | solution.py:23
  29.8 9.9 %collective-permute-start.4 = (f32[18,1,1024]{2,1,0:T(1,128)S(1)}, f32[18,1,1024]{2,1,0:T(1,128)S(1)}, u32[]{:S(2)}, u32[]{:S(2)}) collective-permute-start(f32[18,1,1024]{2,1,0:T(1,128)S(1)} %get-tuple-element.14), channel_id=1, source_target_pairs={{1,0},{2,1},{3,2},{4,3},{5,4},{6,5},{7,6},{8,7},{9,8},{10,9},{11,1... | collective-permute-start | bytes 221192 | tf_op jit(solution)/shard_map/ppermute | solution.py:34
  34.3 8.9 %collective-permute-start.5 = (f32[18,1,1024]{2,1,0:T(1,128)S(1)}, f32[18,1,1024]{2,1,0:T(1,128)S(1)}, u32[]{:S(2)}, u32[]{:S(2)}) collective-permute-start(f32[18,1,1024]{2,1,0:T(1,128)S(1)} %get-tuple-element.15), channel_id=1, source_target_pairs={{0,1},{1,2},{2,3},{3,4},{4,5},{5,6},{6,7},{7,8},{8,9},{9,10},{10,1... | collective-permute-start | bytes 221192 | tf_op jit(solution)/shard_map/ppermute | solution.py:31
  130.6 22.1 %copy-start = (f32[16,8,1024]{2,1,0:T(8,128)}, f32[16,8,1024]{2,1,0:T(8,128)S(1)}, u32[]{:S(2)}) copy-start(f32[16,8,1024]{2,1,0:T(8,128)S(1)} %multiply_add_fusion.4) | copy-start | bytes 1572868
  130.6 7.3 %collective-permute-start.6 = (f32[1,8,1024]{2,1,0:T(8,128)S(1)}, f32[1,8,1024]{2,1,0:T(8,128)S(1)}, u32[]{:S(2)}, u32[]{:S(2)}) collective-permute-start(f32[1,8,1024]{2,1,0:T(8,128)S(1)} %get-tuple-element.27), channel_id=1, source_target_pairs={{16,0},{32,16},{48,32},{64,48},{80,64},{96,80},{112,96},{128,112},... | collective-permute-start | bytes 98312 | tf_op jit(solution)/shard_map/ppermute | solution.py:34
  136.0 5.2 collective-permute-start.7
  141.3 6.2 %collective-permute-start.8 = (f32[18,1,1024]{2,1,0:T(1,128)S(1)}, f32[18,1,1024]{2,1,0:T(1,128)S(1)}, u32[]{:S(2)}, u32[]{:S(2)}) collective-permute-start(f32[18,1,1024]{2,1,0:T(1,128)S(1)} %get-tuple-element.12), channel_id=1, source_target_pairs={{1,0},{2,1},{3,2},{4,3},{5,4},{6,5},{7,6},{8,7},{9,8},{10,9},{11,1... | collective-permute-start | bytes 221192 | tf_op jit(solution)/shard_map/ppermute | solution.py:34
  144.2 8.5 %collective-permute-start.9 = (f32[18,1,1024]{2,1,0:T(1,128)S(1)}, f32[18,1,1024]{2,1,0:T(1,128)S(1)}, u32[]{:S(2)}, u32[]{:S(2)}) collective-permute-start(f32[18,1,1024]{2,1,0:T(1,128)S(1)} %get-tuple-element.13), channel_id=1, source_target_pairs={{0,1},{1,2},{2,3},{3,4},{4,5},{5,6},{6,7},{7,8},{8,9},{9,10},{10,1... | collective-permute-start | bytes 221192 | tf_op jit(solution)/shard_map/ppermute | solution.py:31
  327.6 11.8 %collective-permute-start.10 = (f32[1,8,1024]{2,1,0:T(8,128)S(1)}, f32[1,8,1024]{2,1,0:T(8,128)S(1)}, u32[]{:S(2)}, u32[]{:S(2)}) collective-permute-start(f32[1,8,1024]{2,1,0:T(8,128)S(1)} %get-tuple-element.23), channel_id=1, source_target_pairs={{16,0},{32,16},{48,32},{64,48},{80,64},{96,80},{112,96},{128,112},... | collective-permute-start | bytes 98312 | tf_op jit(solution)/shard_map/ppermute | solution.py:34
  332.6 6.8 %collective-permute-start.11 = (f32[1,8,1024]{2,1,0:T(8,128)S(1)}, f32[1,8,1024]{2,1,0:T(8,128)S(1)}, u32[]{:S(2)}, u32[]{:S(2)}) collective-permute-start(f32[1,8,1024]{2,1,0:T(8,128)S(1)} %get-tuple-element.22), channel_id=1, source_target_pairs={{0,16},{16,32},{32,48},{48,64},{64,80},{80,96},{96,112},{112,128},... | collective-permute-start | bytes 98312 | tf_op jit(solution)/shard_map/ppermute | solution.py:31
  339.5 13.0 %collective-permute-start.12 = (f32[18,1,1024]{2,1,0:T(1,128)S(1)}, f32[18,1,1024]{2,1,0:T(1,128)S(1)}, u32[]{:S(2)}, u32[]{:S(2)}) collective-permute-start(f32[18,1,1024]{2,1,0:T(1,128)S(1)} %get-tuple-element.10), channel_id=1, source_target_pairs={{1,0},{2,1},{3,2},{4,3},{5,4},{6,5},{7,6},{8,7},{9,8},{10,9},{11,1... | collective-permute-start | bytes 221192 | tf_op jit(solution)/shard_map/ppermute | solution.py:34
  345.5 8.4 %collective-permute-start.13 = (f32[18,1,1024]{2,1,0:T(1,128)S(1)}, f32[18,1,1024]{2,1,0:T(1,128)S(1)}, u32[]{:S(2)}, u32[]{:S(2)}) collective-permute-start(f32[18,1,1024]{2,1,0:T(1,128)S(1)} %get-tuple-element.11), channel_id=1, source_target_pairs={{0,1},{1,2},{2,3},{3,4},{4,5},{5,6},{6,7},{7,8},{8,9},{9,10},{10,1... | collective-permute-start | bytes 221192 | tf_op jit(solution)/shard_map/ppermute | solution.py:31
  449.5 69.9 %copy-start.20 = (f32[128,16,64]{0,1,2:T(8,128)S(1)}, f32[128,16,64]{0,1,2:T(8,128)}, u32[]{:S(2)}) copy-start(f32[128,16,64]{0,1,2:T(8,128)} %copy.56) | copy-start | bytes 1572868
  533.2 23.2 %copy-start.9 = (f32[16,8,1024]{2,1,0:T(8,128)}, f32[16,8,1024]{2,1,0:T(8,128)S(1)}, u32[]{:S(2)}) copy-start(f32[16,8,1024]{2,1,0:T(8,128)S(1)} %add_add_fusion) | copy-start | bytes 1572868
  533.2 6.8 %collective-permute-start.14 = (f32[1,8,1024]{2,1,0:T(8,128)S(1)}, f32[1,8,1024]{2,1,0:T(8,128)S(1)}, u32[]{:S(2)}, u32[]{:S(2)}) collective-permute-start(f32[1,8,1024]{2,1,0:T(8,128)S(1)} %get-tuple-element.19), channel_id=1, source_target_pairs={{16,0},{32,16},{48,32},{64,48},{80,64},{96,80},{112,96},{128,112},... | collective-permute-start | bytes 98312 | tf_op jit(solution)/shard_map/ppermute | solution.py:34
  538.1 5.2 collective-permute-start.15
  543.4 6.7 %collective-permute-start.16 = (f32[18,1,1024]{2,1,0:T(1,128)S(1)}, f32[18,1,1024]{2,1,0:T(1,128)S(1)}, u32[]{:S(2)}, u32[]{:S(2)}) collective-permute-start(f32[18,1,1024]{2,1,0:T(1,128)S(1)} %get-tuple-element.8), channel_id=1, source_target_pairs={{1,0},{2,1},{3,2},{4,3},{5,4},{6,5},{7,6},{8,7},{9,8},{10,9},{11,1... | collective-permute-start | bytes 221192 | tf_op jit(solution)/shard_map/ppermute | solution.py:34
  547.9 8.5 %copy-start.11 = (f32[16,8,1024]{2,1,0:T(8,128)S(1)}, f32[16,8,1024]{2,1,0:T(8,128)}, u32[]{:S(2)}) copy-start(f32[16,8,1024]{2,1,0:T(8,128)} %tile.63) | copy-start | bytes 1572868
  547.9 8.5 %copy-start.13 = (f32[16,8,1024]{2,1,0:T(8,128)S(1)}, f32[16,8,1024]{2,1,0:T(8,128)}, u32[]{:S(2)}) copy-start(f32[16,8,1024]{2,1,0:T(8,128)} %tile.67) | copy-start | bytes 1572868
  547.9 8.5 %collective-permute-start.17 = (f32[18,1,1024]{2,1,0:T(1,128)S(1)}, f32[18,1,1024]{2,1,0:T(1,128)S(1)}, u32[]{:S(2)}, u32[]{:S(2)}) collective-permute-start(f32[18,1,1024]{2,1,0:T(1,128)S(1)} %get-tuple-element.9), channel_id=1, source_target_pairs={{0,1},{1,2},{2,3},{3,4},{4,5},{5,6},{6,7},{7,8},{8,9},{9,10},{10,1... | collective-permute-start | bytes 221192 | tf_op jit(solution)/shard_map/ppermute | solution.py:31
  (21 other events, 60.0 us)
